TPU v7x, 512 devices: a whole 4x4x16 slice. The times are simulated.
512 devices in a mesh: pole: 2 (over core), prow: 16 (over z), pcol: 16 (over x, y).
Axes of the slice: x: 4, y: 4, z: 16, core: 2. Of those that a mesh axis runs over, the one named last changes fastest.
Arguments:
- inverse_trailing: float32 [32768, 16384], P(('pole', 'prow'), 'pcol'), parts along dimension 0, may hold values from -6 to 6
- factor_blocks: float32 [6, 4096, 256], P('pole', 'prow'), parts along dimension 0, may hold values from -0.09375 to 0.09375
- diag_pivots: float32 [256, 6, 256], P('pcol', 'pole'), parts along dimension 1, may hold values from -6 to 6
- structure: int32 [3, 16], replicated, may hold values from 0 to 63, as said below
- owner_map: int32 [64], replicated, may hold values from 0 to 63, each once
Outputs:
- row_inverse: float32 [256, 6, 16384], P('pcol', 'pole', 'prow'), parts along dimension 1
- diag_inverse: float32 [256, 6, 256], P('pcol', 'pole'), parts along dimension 1
There are 2 independent parts, one for each index of `pole`. A program takes and returns all parts, laid end to end along the dimension named above; an argument that names none is the same for every part. Nothing has to cross between parts.
Inputs may be any that keep to these rules, and one draw needn't show every extreme that they name: `structure`: each row lists 16 distinct logical ancestor blocks.
All inputs are finite; a program needn't handle non-finite values.
Results may differ from a plain program's by a relative error of at most 0.0001.
Values sent between devices are 32-bit elements; how exact they have to be, the bound alone decides.
No kernel may reach another device: no remote copies, remote signals or barrier semaphores. Data moves between devices by JAX's collectives and lax.ppermute only.
A program may use at most 64 MiB of HBM per device.

v0:
```python
import jax
import jax.numpy as jnp
from jax import lax
from jax.sharding import PartitionSpec as P


def diag_product(values, factor):
    return jnp.einsum("awj,wjb->awb", values, factor, precision=lax.Precision.HIGHEST)


def shards(inverse_trailing, factor_blocks, diag_pivots, structure, owner_map):
    width = factor_blocks.shape[2]
    window = factor_blocks.shape[0]
    owned = inverse_trailing.shape[0] // width
    ancestors = owner_map.shape[0]
    row_index = lax.axis_index("prow")
    col_index = lax.axis_index("pcol")
    catalog = jnp.arange(ancestors, dtype=jnp.int32)
    positions = jnp.sum(
        jnp.where(structure[:, :, None] == catalog[None, None, :], owner_map[None, None, :], 0),
        axis=2,
    )
    slots = jnp.arange(owned, dtype=jnp.int32)
    col_slots = col_index * owned + slots
    row_slots = row_index * owned + slots
    piece = lax.all_gather(factor_blocks, "prow", axis=1, tiled=True)
    count = piece.shape[1] // width
    blocks = piece.reshape(window, count, width, width)
    col_pick = (positions[:, None, :] == col_slots[None, :, None]).astype(jnp.float32)
    row_pick = (positions[:, None, :] == row_slots[None, :, None]).astype(jnp.float32)
    col_acc = jnp.einsum("wsi,wiab->wsab", col_pick, blocks, precision=lax.Precision.HIGHEST)
    row_acc = jnp.einsum("wsi,wiab->wsab", row_pick, blocks, precision=lax.Precision.HIGHEST)
    col_factor = col_acc.reshape(window, owned * width, width)
    row_factor = row_acc.reshape(window, owned * width, width)
    in_rows = jnp.any(positions[:, None, :] == row_slots[None, :, None], axis=2).astype(jnp.float32)
    row_mask = jnp.repeat(in_rows, width, axis=1)
    summed = lax.psum_scatter(
        -jnp.einsum("wja,ij->awi", col_factor, inverse_trailing, precision=lax.Precision.HIGHEST),
        "pcol",
        scatter_dimension=0,
        tiled=True,
    )
    row_inverse = summed * row_mask[None, :, :]
    local_diag = diag_product(row_inverse, row_factor)
    total_diag = lax.psum(local_diag, "prow")
    diag_inverse = diag_pivots - total_diag
    return (row_inverse, diag_inverse)


def solution(mesh):
    in_specs = (
        P(("pole", "prow"), "pcol"),
        P("pole", "prow", None),
        P("pcol", "pole", None),
        P(),
        P(),
    )
    out_specs = (P("pcol", "pole", "prow"), P("pcol", "pole", None))
    return jax.shard_map(shards, mesh=mesh, in_specs=in_specs, out_specs=out_specs, check_vma=False)
```

profile of v0, /device:TPU:2, one launch (start us, length us, event | category | flops | bytes accessed | tf_op | source)
XLA Modules:
  0.0 359.3 jit_solution(15618497550631797289)
XLA Ops:
  7.2 0.0 all-gather.2.cloned.1.call-start
  7.2 0.7 all-gather.2.cloned.1.call-update
  7.9 0.0 reduce-scatter.2.cloned.1.call-start
  8.0 0.9 select_reduce_fusion
  8.9 153.8 %all-gather.2.cloned.1.call-done = f32[3,4096,256]{2,1,0:T(8,128)} async-done(((f32[3,256,256]{2,1,0:T(8,128)}), f32[3,4096,256]{2,1,0:T(8,128)}) %all-gather.2.cloned.1.call-update) | async-done | bytes 12582928 | tf_op jit(solution)/shard_map/all_gather | solution.py:26
  162.6 16.1 %fusion.2 = f32[3,4,256,256]{3,1,2,0:T(4,128)S(1)} fusion(f32[3,16,256,256]{3,2,1,0:T(8,128)} %bitcast.28, s32[3,16]{1,0:T(4,128)S(1)} %select_reduce_fusion, s32[4]{0:T(128)S(1)} %iota_add_fusion.1), kind=kOutput, calls=%fused_computation.2 | convolution fusion | flops 150995136 | bytes 15728848 | tf_op jit(solution)/shard_map/wsi,wiab->wsab/dot_general | solution.py:31
  178.8 0.0 copy-start
  178.8 0.5 copy.13
  179.3 1.6 copy-done
  181.0 22.3 %negate_bitcast_fusion = f32[256,3,1024]{2,0,1:T(8,128)} fusion(f32[3,1024,256]{2,1,0:T(8,128)S(1)} %bitcast.31, f32[1024,1024]{1,0:T(8,128)S(1)} %copy-done), kind=kOutput, calls=%fused_computation.6 | convolution fusion | flops 9664462848 | bytes 10485760 | tf_op jit(solution)/shard_map/wja,ij->awi/dot_general | solution.py:38
  203.3 0.0 reduce-scatter.2.cloned.1.call-update
  203.3 0.2 compare_reduce_fusion
  203.5 0.1 broadcast_bitcast_fusion
  203.6 15.8 %fusion = f32[3,4,256,256]{3,1,2,0:T(4,128)S(1)} fusion(f32[3,16,256,256]{3,2,1,0:T(8,128)} %bitcast.29, s32[3,16]{1,0:T(4,128)S(1)} %select_reduce_fusion, s32[4]{0:T(128)S(1)} %iota_add_fusion), kind=kOutput, calls=%fused_computation | convolution fusion | flops 150995136 | bytes 15728848 | tf_op jit(solution)/shard_map/wsi,wiab->wsab/dot_general | solution.py:32
  219.4 0.5 copy.16
  220.0 0.0 copy-start.2
  220.0 72.0 %reduce-scatter.2.cloned.1.call-done = f32[16,3,1024]{2,0,1:T(8,128)} async-done(((f32[256,3,1024]{2,0,1:T(8,128)}), f32[16,3,1024]{2,0,1:T(8,128)}) %reduce-scatter.2.cloned.1.call-update) | async-done | bytes 196624 | tf_op jit(solution)/shard_map/reduce_scatter | solution.py:37
  292.0 0.9 broadcast_multiply_fusion
  293.0 0.0 copy-start.1
  293.0 1.7 convolution_bitcast_fusion
  294.7 56.9 %psum.7 = f32[16,3,256]{2,0,1:T(8,128)S(1)} all-reduce(f32[16,3,256]{2,0,1:T(8,128)S(1)} %convolution_bitcast_fusion), channel_id=1, replica_groups=mesh['pole'=2,'prow'=16,'pcol'=16] {'prow'}, use_global_device_ids=true, to_apply=%region_3.4 | all-reduce | flops 12288 | bytes 98304 | tf_op jit(solution)/shard_map/psum | solution.py:45
  351.6 0.0 copy-done.2
  351.6 0.6 sub.3
  352.2 0.0 copy-done.1
  (4 shorter events, 0.0 us)
Async XLA Ops:
  7.2 155.5 %all-gather.2.cloned.1.call-start = ((), (), s32[]{:S(2)}) async-start(), calls=%async_computation.1 | async-start | bytes 13369344 | tf_op jit(solution)/shard_map/all_gather | solution.py:26
  7.9 284.1 %reduce-scatter.2.cloned.1.call-start = ((), (), s32[]{:S(2)}) async-start(), calls=%async_computation.2 | async-start | bytes 3342336 | tf_op jit(solution)/shard_map/reduce_scatter | solution.py:37
  178.8 2.2 copy-start
  220.0 131.6 %copy-start.2 = (f32[16,3,256]{2,0,1:T(8,128)S(1)}, f32[16,3,256]{2,0,1:T(8,128)}, u32[]{:S(2)}) copy-start(f32[16,3,256]{2,0,1:T(8,128)} %param.7) | copy-start | bytes 147460
  293.0 59.3 %copy-start.1 = (f32[16,3,1024]{2,0,1:T(8,128)}, f32[16,3,1024]{2,0,1:T(8,128)S(1)}, u32[]{:S(2)}) copy-start(f32[16,3,1024]{2,0,1:T(8,128)S(1)} %broadcast_multiply_fusion) | copy-start | bytes 589828
Sparse Core Ops, SparseCore 0:
  10.1 152.5 all-gather.1
  203.4 88.5 reduce-scatter.1
where the time goes:
time: 365 us; the launch traced here: 359 us
  waiting for transfers between devices  226 us (62%)
  blocking collectives  56.9 us (16%)
  matrix products  56 us (15%)
  between operations  14.4 us (4%)
    all_gather x1, waiting for transfers between devices, shards(): piece = lax.all_gather(factor_blocks, 'prow', axis=1, tiled=True)  154 us
    reduce_scatter x1, waiting for transfers between devices, shards(): lax.psum_scatter(-jnp.einsum('wja,ij->awi', col_factor, inverse_trailing,...  72 us
    psum x1, blocking collectives, shards(): total_diag = lax.psum(local_diag, 'prow')  56.9 us
    dot_general x1, matrix products, shards(): jnp.einsum('wja,ij->awi', col_factor, inverse_trailing, precision=lax.Pre...  22.3 us
    dot_general x1, matrix products, shards(): jnp.einsum('wsi,wiab->wsab', col_pick, blocks, precision=lax.Precision.HI...  16.1 us
    dot_general x1, matrix products, shards(): jnp.einsum('wsi,wiab->wsab', row_pick, blocks, precision=lax.Precision.HI...  15.8 us
  transfers between devices with their start and end apart: 2, of which 2 were waited for; matrix products, arithmetic and copies ran while one was open for 5% of the time, Pallas kernels for 0%

commit v1 on v0

--- a/solution.py
+++ b/solution.py
@@ -42,7 +42,7 @@
     )
     row_inverse = summed * row_mask[None, :, :]
     local_diag = diag_product(row_inverse, row_factor)
-    total_diag = lax.psum(local_diag, "prow")
+    total_diag = jnp.sum(lax.all_gather(local_diag, "prow"), axis=0)
     diag_inverse = diag_pivots - total_diag
     return (row_inverse, diag_inverse)
 

time: 365 us -> 343 us (0.940)
  blocking collectives: 56.9 us -> 34.8 us
    psum x1 -> x0, blocking collectives: 56.9 us -> none  [shards(): total_diag = lax.psum(local_diag, 'prow')]
    all_gather x0 -> x1, blocking collectives: none -> 34.8 us  [shards(): total_diag = jnp.sum(lax.all_gather(local_diag, 'prow'), axis=0)]
where the time goes in v1:
time: 343 us; the launch traced here: 337 us
  waiting for transfers between devices  226 us (66%)
  matrix products  56 us (16%)
  blocking collectives  34.8 us (10%)
  between operations  14.4 us (4%)
    all_gather x1, waiting for transfers between devices, shards(): piece = lax.all_gather(factor_blocks, 'prow', axis=1, tiled=True)  154 us
    reduce_scatter x1, waiting for transfers between devices, shards(): lax.psum_scatter(-jnp.einsum('wja,ij->awi', col_factor, inverse_trailing,...  72 us
    all_gather x1, blocking collectives, shards(): total_diag = jnp.sum(lax.all_gather(local_diag, 'prow'), axis=0)  34.8 us
    dot_general x1, matrix products, shards(): jnp.einsum('wja,ij->awi', col_factor, inverse_trailing, precision=lax.Pre...  22.3 us
    dot_general x1, matrix products, shards(): jnp.einsum('wsi,wiab->wsab', col_pick, blocks, precision=lax.Precision.HI...  16.1 us
    dot_general x1, matrix products, shards(): jnp.einsum('wsi,wiab->wsab', row_pick, blocks, precision=lax.Precision.HI...  15.8 us
  transfers between devices with their start and end apart: 2, of which 2 were waited for; matrix products, arithmetic and copies ran while one was open for 5% of the time, Pallas kernels for 0%

profile of v1, /device:TPU:2, one launch (start us, length us, event | category | flops | bytes accessed | tf_op | source)
XLA Modules:
  0.0 337.3 jit_solution(7485519224508859698)
XLA Ops:
  7.2 0.0 all-gather.3.cloned.1.call-start
  7.2 0.7 all-gather.3.cloned.1.call-update
  7.9 0.0 reduce-scatter.2.cloned.1.call-start
  8.0 0.9 select_reduce_fusion
  8.9 153.8 %all-gather.3.cloned.1.call-done = f32[3,4096,256]{2,1,0:T(8,128)} async-done(((f32[3,256,256]{2,1,0:T(8,128)}), f32[3,4096,256]{2,1,0:T(8,128)}) %all-gather.3.cloned.1.call-update) | async-done | bytes 12582928 | tf_op jit(solution)/shard_map/all_gather | solution.py:26
  162.6 16.1 %fusion.2 = f32[3,4,256,256]{3,1,2,0:T(4,128)S(1)} fusion(f32[3,16,256,256]{3,2,1,0:T(8,128)} %bitcast.29, s32[3,16]{1,0:T(4,128)S(1)} %select_reduce_fusion, s32[4]{0:T(128)S(1)} %iota_add_fusion.1), kind=kOutput, calls=%fused_computation.2 | convolution fusion | flops 150995136 | bytes 15728848 | tf_op jit(solution)/shard_map/wsi,wiab->wsab/dot_general | solution.py:31
  178.8 0.0 copy-start
  178.8 0.5 copy.13
  179.3 1.6 copy-done
  181.0 22.3 %negate_bitcast_fusion = f32[256,3,1024]{2,0,1:T(8,128)} fusion(f32[3,1024,256]{2,1,0:T(8,128)S(1)} %bitcast.32, f32[1024,1024]{1,0:T(8,128)S(1)} %copy-done), kind=kOutput, calls=%fused_computation.6 | convolution fusion | flops 9664462848 | bytes 10485760 | tf_op jit(solution)/shard_map/wja,ij->awi/dot_general | solution.py:38
  203.3 0.0 reduce-scatter.2.cloned.1.call-update
  203.3 0.2 compare_reduce_fusion
  203.5 0.1 broadcast_bitcast_fusion
  203.6 15.8 %fusion = f32[3,4,256,256]{3,1,2,0:T(4,128)S(1)} fusion(f32[3,16,256,256]{3,2,1,0:T(8,128)} %bitcast.30, s32[3,16]{1,0:T(4,128)S(1)} %select_reduce_fusion, s32[4]{0:T(128)S(1)} %iota_add_fusion), kind=kOutput, calls=%fused_computation | convolution fusion | flops 150995136 | bytes 15728848 | tf_op jit(solution)/shard_map/wsi,wiab->wsab/dot_general | solution.py:32
  219.4 0.5 copy.16
  220.0 0.0 copy-start.2
  220.0 72.0 %reduce-scatter.2.cloned.1.call-done = f32[16,3,1024]{2,0,1:T(8,128)} async-done(((f32[256,3,1024]{2,0,1:T(8,128)}), f32[16,3,1024]{2,0,1:T(8,128)}) %reduce-scatter.2.cloned.1.call-update) | async-done | bytes 196624 | tf_op jit(solution)/shard_map/reduce_scatter | solution.py:37
  292.0 0.9 broadcast_multiply_fusion
  293.0 0.0 copy-start.1
  293.0 1.7 convolution_bitcast_fusion
  294.7 34.8 %all-gather = f32[256,3,256]{2,0,1:T(8,128)S(1)} all-gather(f32[16,3,256]{2,0,1:T(8,128)S(1)} %convolution_bitcast_fusion), channel_id=2, replica_groups=mesh['pole'=2,'prow'=16,'pcol'=16] {'prow'}, dimensions={0}, use_global_device_ids=true | all-gather | bytes 835584 | tf_op jit(solution)/shard_map/all_gather | solution.py:45
  329.6 0.1 reduce_sum.19
  329.6 0.0 copy-done.2
  329.7 0.6 sub.3
  (5 shorter events, 0.0 us)
Async XLA Ops:
  7.2 155.5 %all-gather.3.cloned.1.call-start = ((), (), s32[]{:S(2)}) async-start(), calls=%async_computation.1 | async-start | bytes 13369344 | tf_op jit(solution)/shard_map/all_gather | solution.py:26
  7.9 284.1 %reduce-scatter.2.cloned.1.call-start = ((), (), s32[]{:S(2)}) async-start(), calls=%async_computation.2 | async-start | bytes 3342336 | tf_op jit(solution)/shard_map/reduce_scatter | solution.py:37
  178.8 2.2 copy-start
  220.0 109.6 %copy-start.2 = (f32[16,3,256]{2,0,1:T(8,128)S(1)}, f32[16,3,256]{2,0,1:T(8,128)}, u32[]{:S(2)}) copy-start(f32[16,3,256]{2,0,1:T(8,128)} %param.7) | copy-start | bytes 147460
  293.0 37.3 %copy-start.1 = (f32[16,3,1024]{2,0,1:T(8,128)}, f32[16,3,1024]{2,0,1:T(8,128)S(1)}, u32[]{:S(2)}) copy-start(f32[16,3,1024]{2,0,1:T(8,128)S(1)} %broadcast_multiply_fusion) | copy-start | bytes 589828
Sparse Core Ops, SparseCore 0:
  10.1 152.5 all-gather.2
  203.4 88.5 reduce-scatter.1

commit v2 on v0

--- a/solution.py
+++ b/solution.py
@@ -23,7 +23,9 @@
     slots = jnp.arange(owned, dtype=jnp.int32)
     col_slots = col_index * owned + slots
     row_slots = row_index * owned + slots
-    piece = lax.all_gather(factor_blocks, "prow", axis=1, tiled=True)
+    piece = jnp.concatenate(
+        lax.all_to_all(jnp.stack([factor_blocks] * lax.axis_size("prow")), "prow", 0, 0), axis=1
+    )
     count = piece.shape[1] // width
     blocks = piece.reshape(window, count, width, width)
     col_pick = (positions[:, None, :] == col_slots[None, :, None]).astype(jnp.float32)

time: 365 us -> 776 us (2.13)
  waiting for transfers between devices: 226 us -> 616 us
  starting transfers between devices: 0.08 us -> 15.4 us
    all_to_all x0 -> x1, waiting for transfers between devices: none -> 542 us  [shards(): lax.all_to_all(jnp.stack([factor_blocks] * lax.axis_size('prow')), 'prow'...]
    all_gather x1 -> x0, waiting for transfers between devices: 154 us -> none  [shards(): piece = lax.all_gather(factor_blocks, 'prow', axis=1, tiled=True)]
    all_to_all x0 -> x1, starting transfers between devices: none -> 15.4 us  [shards(): lax.all_to_all(jnp.stack([factor_blocks] * lax.axis_size('prow')), 'prow'...]
  transfers between devices with their start and end apart: 2 -> 2, of which waited for: 2 -> 2; matrix products, arithmetic and copies ran while one was open for 5% -> 2% of each run, Pallas kernels for 0% -> 0%
where the time goes in v2:
time: 776 us; the launch traced here: 770 us
  waiting for transfers between devices  616 us (79%)
  blocking collectives  56.9 us (7%)
  matrix products  56 us (7%)
  starting transfers between devices  15.4 us (2%)
  between operations  14.4 us (2%)
  local copies, waits for them, and re-layouts  9.91 us (1%)
    all_to_all x1, waiting for transfers between devices, shards(): lax.all_to_all(jnp.stack([factor_blocks] * lax.axis_size('prow')), 'prow'...  542 us
    reduce_scatter x1, waiting for transfers between devices, shards(): lax.psum_scatter(-jnp.einsum('wja,ij->awi', col_factor, inverse_trailing,...  74 us
    psum x1, blocking collectives, shards(): total_diag = lax.psum(local_diag, 'prow')  56.9 us
    dot_general x1, matrix products, shards(): jnp.einsum('wja,ij->awi', col_factor, inverse_trailing, precision=lax.Pre...  22.3 us
    dot_general x1, matrix products, shards(): jnp.einsum('wsi,wiab->wsab', col_pick, blocks, precision=lax.Precision.HI...  16.1 us
    dot_general x1, matrix products, shards(): jnp.einsum('wsi,wiab->wsab', row_pick, blocks, precision=lax.Precision.HI...  15.9 us
  transfers between devices with their start and end apart: 2, of which 2 were waited for; matrix products, arithmetic and copies ran while one was open for 2% of the time, Pallas kernels for 0%

profile of v2, /device:TPU:2, one launch (start us, length us, event | category | flops | bytes accessed | tf_op | source)
XLA Modules:
  0.0 770.1 jit_solution(17285341397212428059)
XLA Ops:
  7.2 7.1 stack.2
  14.3 15.4 %all-to-all-start = ((f32[16,3,256,256]{3,2,1,0:T(8,128)}), f32[16,3,256,256]{3,2,1,0:T(8,128)}, u32[]{:S(2)}, u32[]{:S(2)}) async-start(f32[16,3,256,256]{3,2,1,0:T(8,128)} %stack.2), calls=%async_computation | async-start | bytes 25165824 | tf_op jit(solution)/shard_map/all_to_all | solution.py:27
  29.6 0.0 reduce-scatter.2.cloned.1.call-start
  29.7 0.0 copy-done.3
  29.7 0.0 copy-done.4
  29.7 0.2 select_reduce_fusion
  29.9 541.5 %all-to-all-done = f32[16,3,256,256]{3,2,1,0:T(8,128)} async-done(((f32[16,3,256,256]{3,2,1,0:T(8,128)}), f32[16,3,256,256]{3,2,1,0:T(8,128)}, u32[]{:S(2)}, u32[]{:S(2)}) %all-to-all-start) | async-done | bytes 12582944 | tf_op jit(solution)/shard_map/all_to_all | solution.py:27
  571.5 16.1 %fusion.2 = f32[3,4,256,256]{3,1,2,0:T(4,128)S(1)} fusion(f32[16,3,256,256]{3,2,1,0:T(8,128)} %all-to-all-done, s32[3,16]{1,0:T(4,128)S(1)} %select_reduce_fusion, s32[4]{0:T(128)S(1)} %iota_add_fusion.1), kind=kOutput, calls=%fused_computation.2 | convolution fusion | flops 150995136 | bytes 15728848 | tf_op jit(solution)/shard_map/wsi,wiab->wsab/dot_general | solution.py:33
  587.6 0.0 copy-start
  587.6 0.5 copy.15
  588.1 1.6 copy-done
  589.8 22.3 %negate_bitcast_fusion = f32[256,3,1024]{2,0,1:T(8,128)} fusion(f32[3,1024,256]{2,1,0:T(8,128)S(1)} %bitcast.33, f32[1024,1024]{1,0:T(8,128)S(1)} %copy-done), kind=kOutput, calls=%fused_computation.8 | convolution fusion | flops 9664462848 | bytes 10485760 | tf_op jit(solution)/shard_map/wja,ij->awi/dot_general | solution.py:40
  612.1 0.0 reduce-scatter.2.cloned.1.call-update
  612.1 0.2 compare_reduce_fusion
  612.3 0.1 broadcast_bitcast_fusion
  612.4 15.9 %fusion = f32[3,4,256,256]{3,1,2,0:T(4,128)S(1)} fusion(f32[16,3,256,256]{3,2,1,0:T(8,128)} %all-to-all-done, s32[3,16]{1,0:T(4,128)S(1)} %select_reduce_fusion, s32[4]{0:T(128)S(1)} %iota_add_fusion), kind=kOutput, calls=%fused_computation | convolution fusion | flops 150995136 | bytes 15728848 | tf_op jit(solution)/shard_map/wsi,wiab->wsab/dot_general | solution.py:34
  628.3 0.5 copy.17
  628.8 0.0 copy-start.2
  628.8 74.0 %reduce-scatter.2.cloned.1.call-done = f32[16,3,1024]{2,0,1:T(8,128)} async-done(((f32[256,3,1024]{2,0,1:T(8,128)}), f32[16,3,1024]{2,0,1:T(8,128)}) %reduce-scatter.2.cloned.1.call-update) | async-done | bytes 196624 | tf_op jit(solution)/shard_map/reduce_scatter | solution.py:39
  702.8 0.9 broadcast_multiply_fusion
  703.8 0.0 copy-start.1
  703.8 1.7 convolution_bitcast_fusion
  705.5 56.9 %psum.7 = f32[16,3,256]{2,0,1:T(8,128)S(1)} all-reduce(f32[16,3,256]{2,0,1:T(8,128)S(1)} %convolution_bitcast_fusion), channel_id=1, replica_groups=mesh['pole'=2,'prow'=16,'pcol'=16] {'prow'}, use_global_device_ids=true, to_apply=%region_3.4 | all-reduce | flops 12288 | bytes 98304 | tf_op jit(solution)/shard_map/psum | solution.py:47
  762.4 0.6 sub.3
  (8 shorter events, 0.0 us)
Async XLA Ops:
  14.3 15.5 %copy-start.3 = (s32[3,16]{1,0:T(4,128)S(1)}, s32[3,16]{1,0:T(4,128)}, u32[]{:S(2)}) copy-start(s32[3,16]{1,0:T(4,128)} %param.8) | copy-start | bytes 580
  14.3 15.5 %copy-start.4 = (s32[64]{0:T(128)S(1)}, s32[64]{0:T(128)}, u32[]{:S(2)}) copy-start(s32[64]{0:T(128)} %param.9) | copy-start | bytes 772
  14.3 557.2 %all-to-all-start = ((f32[16,3,256,256]{3,2,1,0:T(8,128)}), f32[16,3,256,256]{3,2,1,0:T(8,128)}, u32[]{:S(2)}, u32[]{:S(2)}) async-start(f32[16,3,256,256]{3,2,1,0:T(8,128)} %stack.2), calls=%async_computation | async-start | bytes 25165824 | tf_op jit(solution)/shard_map/all_to_all | solution.py:27
  29.6 673.2 %reduce-scatter.2.cloned.1.call-start = ((), (), s32[]{:S(2)}) async-start(), calls=%async_computation.2 | async-start | bytes 3342336 | tf_op jit(solution)/shard_map/reduce_scatter | solution.py:39
  587.6 2.2 copy-start
  628.8 133.6 %copy-start.2 = (f32[16,3,256]{2,0,1:T(8,128)S(1)}, f32[16,3,256]{2,0,1:T(8,128)}, u32[]{:S(2)}) copy-start(f32[16,3,256]{2,0,1:T(8,128)} %param.7) | copy-start | bytes 147460
  703.8 59.3 %copy-start.1 = (f32[16,3,1024]{2,0,1:T(8,128)}, f32[16,3,1024]{2,0,1:T(8,128)S(1)}, u32[]{:S(2)}) copy-start(f32[16,3,1024]{2,0,1:T(8,128)S(1)} %broadcast_multiply_fusion) | copy-start | bytes 589828
Sparse Core Ops, SparseCore 0:
  612.2 90.5 reduce-scatter.1
